TPU v7x, 256 devices: a whole 4x4x8 slice. The times are simulated.
256 devices in a mesh: ctx: 32 (over y, z_hi, x), uly: 8 (over z_lo, core).
Axes of the slice: x: 4, y: 4, z: 8 (z_hi: 2, z_lo: 4; z = z_hi * 4 + z_lo), core: 2. Of those that a mesh axis runs over, the one named last changes fastest.
Arguments:
- queries: bfloat16 [32768, 4096], P(('ctx', 'uly')), may hold values from -5 to 5
- keys: bfloat16 [32768, 1024], P(('ctx', 'uly')), may hold values from -5 to 5
- values: bfloat16 [32768, 1024], P(('ctx', 'uly')), may hold values from -6 to 6
- output_gradient: bfloat16 [32768, 4096], P(('ctx', 'uly')), may hold values from -6 to 6
- doc_lengths: int32 [32], replicated, may hold values from 1 to 3072, 32768 in all
Outputs:
- grad_queries: bfloat16 [32768, 4096], P(('ctx', 'uly'))
- keys_gradient: bfloat16 [32768, 1024], P(('ctx', 'uly'))
- values_gradient: bfloat16 [32768, 1024], P(('ctx', 'uly'))
Inputs may be any that keep to these rules, and one draw needn't show every extreme that they name: `doc_lengths`: whole documents that fill the sequence; the longest is exactly 3072 tokens.
All inputs are finite; a program needn't handle non-finite values.
Results may differ from a plain program's by a relative error of at most 0.017.
Values may be sent and summed in bfloat16 or wider, within the bound.
No kernel may reach another device: no remote copies, remote signals or barrier semaphores. Data moves between devices by JAX's collectives and lax.ppermute only.
A program may use at most 64 MiB of HBM per device.

v0:
```python
import functools
import math

import jax
import jax.numpy as jnp
from jax import lax
from jax.experimental import pallas as pl
from jax.experimental.pallas import tpu as pltpu
from jax.sharding import PartitionSpec as P

HEAD_SIZE = 128
REACH = 3
Q_BLOCK = 512
K_BLOCK = 512

NEG = -1e30


def mirror_of(uly, cores):
    run = uly // cores
    return [(run - 1 - u // cores) * cores + u % cores for u in range(uly)]


def from_behind(shard, by, flips, cores):
    ctx = lax.axis_size("ctx")
    uly = lax.axis_size("uly")
    mirror = mirror_of(uly, cores)
    pairs = []
    for c in range(ctx):
        d = c + by
        if not 0 <= d < ctx:
            continue
        for u in range(uly):
            group = mirror[u] if flips[c] else u
            pairs.append((c * uly + u, d * uly + (mirror[group] if flips[d] else group)))
    return lax.ppermute(shard, ("ctx", "uly"), pairs)


def mirrored(x, flip, cores):
    rows, uly = x.shape[0], x.shape[1]
    split = x.reshape(rows, uly // cores, cores, x.shape[2])
    return jnp.where(flip, split[:, ::-1], split).reshape(x.shape)


def attention_kernel(
    meta_ref, q_ref, do_ref, k_ref, v_ref, qs_ref, qsr_ref,
    dq_ref, dkv_ref,
    m_s, l_s, acc_s, lse_s, delta_s, dq_s,
    *, groups, q_blocks, scale,
):
    T, TK, D = Q_BLOCK, K_BLOCK, HEAD_SIZE
    nt = (((1,), (1,)), ((), ()))
    dkv_ref[...] = jnp.zeros_like(dkv_ref)
    q_base = meta_ref[0]
    k_base = meta_ref[1]

    def q_block(qb, carry):
        q0 = pl.multiple_of(qb * T, T)
        lo = meta_ref[2 + 3 * qb]
        hi = meta_ref[3 + 3 * qb]
        last_start = meta_ref[4 + 3 * qb]
        m_s[...] = jnp.full_like(m_s, NEG)
        l_s[...] = jnp.zeros_like(l_s)
        acc_s[...] = jnp.zeros_like(acc_s)

        def tile_mask(k0):
            k_pos = k_base + k0 + lax.broadcasted_iota(jnp.int32, (TK, T), 0)
            q_pos = q_base + q0 + lax.broadcasted_iota(jnp.int32, (TK, T), 1)
            start = qsr_ref[:, pl.ds(q0, T)]
            return (k_pos <= q_pos) & (k_pos >= start)

        def is_full(k0):
            return (k_base + k0 + TK - 1 <= q_base + q0) & (k_base + k0 >= last_start)

        def fwd_tile(k0, masked):
            k = k_ref[pl.ds(k0, TK), :]
            v_t = v_ref[pl.ds(k0, TK), :].astype(jnp.float32).T.astype(jnp.bfloat16)
            mask = tile_mask(k0) if masked else None
            for h in range(groups):
                qh = q_ref[pl.ds(q0, T), pl.ds(h * D, D)]
                raw = lax.dot_general(k, qh, nt, preferred_element_type=jnp.float32) * scale
                s = jnp.where(mask, raw, NEG) if masked else raw
                old_high = m_s[h]
                new_high = jnp.maximum(old_high, jnp.max(s, axis=0, keepdims=True))
                factor = jnp.exp(old_high - new_high)
                terms = jnp.exp(s - new_high)
                l_s[h] = l_s[h] * factor + jnp.sum(terms, axis=0, keepdims=True)
                acc_s[h] = acc_s[h] * factor + jnp.dot(
                    v_t, terms.astype(jnp.bfloat16), preferred_element_type=jnp.float32
                )
                m_s[h] = new_high

        def fwd(kb, c):
            k0 = pl.multiple_of(kb * TK, TK)
            full = is_full(k0)
            pl.when(full)(lambda: fwd_tile(k0, False))
            pl.when(jnp.logical_not(full))(lambda: fwd_tile(k0, True))
            return c

        lax.fori_loop(lo, hi, fwd, 0)
        for h in range(groups):
            total = l_s[h]
            lse_s[h] = m_s[h] + jnp.log(total)
            out = (acc_s[h] / total).astype(jnp.bfloat16).astype(jnp.float32)
            g = do_ref[pl.ds(q0, T), pl.ds(h * D, D)].astype(jnp.float32).T
            delta_s[h] = jnp.sum(g * out, axis=0, keepdims=True)
        dq_s[...] = jnp.zeros_like(dq_s)

        def bwd_tile(k0, masked):
            k = k_ref[pl.ds(k0, TK), :]
            v = v_ref[pl.ds(k0, TK), :]
            k_t = k.astype(jnp.float32).T.astype(jnp.bfloat16)
            mask = tile_mask(k0) if masked else None
            add_k = jnp.zeros((TK, D), jnp.float32)
            add_v = jnp.zeros((TK, D), jnp.float32)
            for h in range(groups):
                qh = q_ref[pl.ds(q0, T), pl.ds(h * D, D)]
                gh = do_ref[pl.ds(q0, T), pl.ds(h * D, D)]
                raw = lax.dot_general(k, qh, nt, preferred_element_type=jnp.float32) * scale
                probs = jnp.exp(raw - lse_s[h])
                if masked:
                    probs = jnp.where(mask, probs, 0.0)
                dprobs = lax.dot_general(v, gh, nt, preferred_element_type=jnp.float32)
                dscores = (probs * (dprobs - delta_s[h])).astype(jnp.bfloat16)
                add_v = add_v + jnp.dot(
                    probs.astype(jnp.bfloat16), gh, preferred_element_type=jnp.float32
                )
                add_k = add_k + jnp.dot(dscores, qh, preferred_element_type=jnp.float32)
                dq_s[h] = dq_s[h] + jnp.dot(k_t, dscores, preferred_element_type=jnp.float32)
            dkv_ref[pl.ds(k0, TK), pl.ds(0, D)] = dkv_ref[pl.ds(k0, TK), pl.ds(0, D)] + add_k
            dkv_ref[pl.ds(k0, TK), pl.ds(D, D)] = dkv_ref[pl.ds(k0, TK), pl.ds(D, D)] + add_v

        def bwd(kb, c):
            k0 = pl.multiple_of(kb * TK, TK)
            full = is_full(k0)
            pl.when(full)(lambda: bwd_tile(k0, False))
            pl.when(jnp.logical_not(full))(lambda: bwd_tile(k0, True))
            return c

        lax.fori_loop(lo, hi, bwd, 0)
        for h in range(groups):
            dq_ref[pl.ds(q0, T), pl.ds(h * D, D)] = (scale * dq_s[h].T).astype(dq_ref.dtype)
        return carry

    lax.fori_loop(0, q_blocks, q_block, 0)


def attend(meta, queries, gradient, key_window, value_window, q_start, groups, scale):
    rows = queries.shape[0]
    width = key_window.shape[0]
    q_blocks = rows // Q_BLOCK
    vmem = pltpu.MemorySpace.VMEM
    kernel = functools.partial(
        attention_kernel, groups=groups, q_blocks=q_blocks, scale=scale
    )
    return pl.pallas_call(
        kernel,
        out_shape=(
            jax.ShapeDtypeStruct(queries.shape, jnp.bfloat16),
            jax.ShapeDtypeStruct((width, 2 * HEAD_SIZE), jnp.float32),
        ),
        in_specs=[pl.BlockSpec(memory_space=pltpu.MemorySpace.SMEM)]
        + [pl.BlockSpec(memory_space=vmem)] * 6,
        out_specs=[pl.BlockSpec(memory_space=vmem)] * 2,
        scratch_shapes=[
            pltpu.VMEM((groups, 1, Q_BLOCK), jnp.float32),
            pltpu.VMEM((groups, 1, Q_BLOCK), jnp.float32),
            pltpu.VMEM((groups, HEAD_SIZE, Q_BLOCK), jnp.float32),
            pltpu.VMEM((groups, 1, Q_BLOCK), jnp.float32),
            pltpu.VMEM((groups, 1, Q_BLOCK), jnp.float32),
            pltpu.VMEM((groups, HEAD_SIZE, Q_BLOCK), jnp.float32),
        ],
        compiler_params=pltpu.CompilerParams(vmem_limit_bytes=48 * 1024 * 1024),
    )(meta, queries, gradient, key_window, value_window, q_start, q_start.reshape(1, rows))


def on_device(queries, keys, values, output_gradient, doc_lengths, flips, cores):
    uly = lax.axis_size("uly")
    ctx_index = lax.axis_index("ctx")
    flip = jnp.asarray(flips)[ctx_index]
    tokens = queries.shape[0]
    q_cols = queries.shape[1] // uly
    kv_cols = keys.shape[1] // uly
    kv = jnp.concatenate(
        [keys.reshape(tokens, uly, kv_cols), values.reshape(tokens, uly, kv_cols)], axis=2
    )
    kv = lax.all_to_all(mirrored(kv, flip, cores), "uly", split_axis=1, concat_axis=0, tiled=True)
    rows = kv.shape[0]
    kv = kv.reshape(rows, 2 * kv_cols)
    window = [kv]
    for step in range(1, REACH + 1):
        window.append(from_behind(kv, step, flips, cores))
    packed = jnp.concatenate(
        [queries.reshape(tokens, uly, q_cols), output_gradient.reshape(tokens, uly, q_cols)],
        axis=2,
    )
    packed = mirrored(packed, flip, cores)
    packed = lax.all_to_all(packed, "uly", split_axis=1, concat_axis=0, tiled=True)
    packed = packed.reshape(rows, 2 * q_cols)
    queries = packed[:, :q_cols]
    gradient = packed[:, q_cols:]
    groups = q_cols // HEAD_SIZE
    softmax_scale = 1.0 / math.sqrt(HEAD_SIZE)

    window = jnp.concatenate(window[::-1], axis=0)
    key_window = window[:, :HEAD_SIZE]
    value_window = window[:, HEAD_SIZE:]

    q_base = ctx_index * rows
    k_base = (ctx_index - REACH) * rows
    q_pos = q_base + jnp.arange(rows, dtype=jnp.int32)
    ends = jnp.cumsum(doc_lengths)
    q_start = jnp.sum(
        jnp.where(ends[None, :] <= q_pos[:, None], doc_lengths[None, :], 0), axis=1
    ).astype(jnp.int32)
    first_rows = jnp.arange(0, rows, Q_BLOCK, dtype=jnp.int32)
    lo = jnp.maximum((q_start[first_rows] - k_base) // K_BLOCK, 0)
    hi = (q_base + first_rows + Q_BLOCK - 1 - k_base) // K_BLOCK + 1
    meta = jnp.concatenate(
        [jnp.stack([q_base, k_base]).astype(jnp.int32), jnp.stack([lo, hi, q_start[first_rows + Q_BLOCK - 1]], axis=1).reshape(-1)]
    ).astype(jnp.int32)

    dq, partials = attend(
        meta, queries, gradient, key_window, value_window, q_start[:, None], groups, softmax_scale
    )
    returned = [
        from_behind(
            partials[(REACH - step) * rows : (REACH - step + 1) * rows].astype(jnp.bfloat16),
            -step,
            flips,
            cores,
        )
        for step in range(1, REACH + 1)
    ]
    out_q = lax.all_to_all(dq, "uly", split_axis=0, concat_axis=1, tiled=True)
    out_q, returned = lax.optimization_barrier((out_q, returned))
    out_q = mirrored(out_q.reshape(out_q.shape[0], uly, q_cols), flip, cores)
    total = partials[REACH * rows :]
    for piece in returned:
        total = total + piece.astype(jnp.float32)
    out_k = (softmax_scale * total[:, :HEAD_SIZE]).astype(jnp.bfloat16)
    out_v = total[:, HEAD_SIZE:].astype(jnp.bfloat16)
    out_kv = lax.all_to_all(
        jnp.concatenate([out_k, out_v], axis=1), "uly", split_axis=0, concat_axis=1, tiled=True
    )
    out_kv = mirrored(out_kv.reshape(out_kv.shape[0], uly, 2 * kv_cols), flip, cores)
    return (
        out_q.reshape(out_q.shape[0], uly * q_cols),
        out_kv[:, :, :kv_cols].reshape(out_kv.shape[0], uly * kv_cols),
        out_kv[:, :, kv_cols:].reshape(out_kv.shape[0], uly * kv_cols),
    )


def layout_of(mesh):
    devices = mesh.devices
    cores = len({getattr(d, "core_on_chip", 0) for d in devices.flat})
    run = devices.shape[1] // cores
    coords = [getattr(devices[c, 0], "coords", None) for c in range(devices.shape[0])]
    if any(xyz is None for xyz in coords):
        return (False,) * devices.shape[0], cores
    return tuple(bool((xyz[2] // run) % 2) for xyz in coords), cores


def solution(mesh):
    flips, cores = layout_of(mesh)
    return jax.shard_map(
        functools.partial(on_device, flips=flips, cores=cores),
        mesh=mesh,
        in_specs=(
            P(("ctx", "uly"), None),
            P(("ctx", "uly"), None),
            P(("ctx", "uly"), None),
            P(("ctx", "uly"), None),
            P(),
        ),
        out_specs=(P(("ctx", "uly"), None), P(("ctx", "uly"), None), P(("ctx", "uly"), None)),
        check_vma=False,
    )
```

profile of v0, /device:TPU:22, one launch (start us, length us, event | category | flops | bytes accessed | tf_op | source)
XLA Modules:
  0.0 305.7 jit_solution(1540638043080859122)
XLA Ops:
  0.6 1.1 concatenate.29
  1.8 0.2 constant_dynamic-update-slice_fusion.3
  1.9 0.0 copy-start.1
  2.0 1.2 concatenate.30
  3.2 1.3 dynamic_slice.3
  4.4 0.4 constant_dynamic-update-slice_fusion.2
  4.8 1.2 broadcast_select_fusion.2
  6.0 0.9 copy.27
  6.9 5.9 %all-to-all-start.1 = ((bf16[128,8,256]{2,0,1:T(8,128)(2,1)}), bf16[128,8,256]{2,0,1:T(8,128)(2,1)}, u32[]{:S(2)}, u32[]{:S(2)}) async-start(bf16[128,8,256]{2,0,1:T(8,128)(2,1)} %bitcast.14), calls=%async_computation.1 | async-start | bytes 1048576 | tf_op jit(solution)/shard_map/all_to_all | solution.py:187
  12.8 0.0 copy-done.1
  12.8 0.8 concatenate.26
  13.6 1.2 constant_dynamic-update-slice_fusion.1
  14.8 1.8 concatenate.27
  16.6 0.9 constant_dynamic-update-slice_fusion
  17.6 2.8 broadcast_select_fusion
  20.4 2.5 copy.26
  22.8 5.4 %all-to-all-done.1 = bf16[128,8,256]{2,0,1:T(8,128)(2,1)} async-done(((bf16[128,8,256]{2,0,1:T(8,128)(2,1)}), bf16[128,8,256]{2,0,1:T(8,128)(2,1)}, u32[]{:S(2)}, u32[]{:S(2)}) %all-to-all-start.1) | async-done | bytes 524320 | tf_op jit(solution)/shard_map/all_to_all | solution.py:187
  28.2 0.0 copy-start.2
  28.2 4.5 %all-to-all-start = ((bf16[128,8,1024]{2,0,1:T(8,128)(2,1)}), bf16[128,8,1024]{2,0,1:T(8,128)(2,1)}, u32[]{:S(2)}, u32[]{:S(2)}) async-start(bf16[128,8,1024]{2,0,1:T(8,128)(2,1)} %bitcast.8), calls=%async_computation | async-start | bytes 4194304 | tf_op jit(solution)/shard_map/all_to_all | solution.py:198
  32.7 0.0 copy-done.2
  32.8 0.1 copy.24
  32.8 0.1 reduce-window.8
  32.9 0.1 reduce
  33.1 0.1 select_reduce_fusion
  33.2 0.6 gather_fusion.1
  33.8 0.6 gather_fusion
  34.4 7.6 %collective-permute-start.2 = (bf16[1024,256]{1,0:T(8,128)(2,1)}, bf16[1024,256]{1,0:T(8,128)(2,1)S(1)}, u32[]{:S(2)}, u32[]{:S(2)}) collective-permute-start(bf16[1024,256]{1,0:T(8,128)(2,1)} %bitcast.17), channel_id=1, source_target_pairs={{0,8},{1,9},{2,10},{3,11},{4,12},{5,13},{6,14},{7,15},{8,16},{9,17... | collective-permute-start | bytes 1572872 | tf_op jit(solution)/shard_map/ppermute | solution.py:36
  42.0 4.3 %collective-permute-start.1 = (bf16[1024,256]{1,0:T(8,128)(2,1)}, bf16[1024,256]{1,0:T(8,128)(2,1)S(1)}, u32[]{:S(2)}, u32[]{:S(2)}) collective-permute-start(bf16[1024,256]{1,0:T(8,128)(2,1)} %bitcast.17), channel_id=1, source_target_pairs={{0,16},{1,17},{2,18},{3,19},{4,20},{5,21},{6,22},{7,23},{8,24},{9,... | collective-permute-start | bytes 1572872 | tf_op jit(solution)/shard_map/ppermute | solution.py:36
  46.3 1.9 collective-permute-start
  48.3 0.1 copy.25
  48.4 0.1 reshape.228
  48.5 0.2 copy.28.qs_ref
  48.7 0.1 pad_add_fusion.1.meta_ref
  48.8 10.6 %collective-permute-done.2 = bf16[1024,256]{1,0:T(8,128)(2,1)S(1)} collective-permute-done((bf16[1024,256]{1,0:T(8,128)(2,1)}, bf16[1024,256]{1,0:T(8,128)(2,1)S(1)}, u32[]{:S(2)}, u32[]{:S(2)}) %collective-permute-start.2) | collective-permute-done | bytes 524320 | tf_op jit(solution)/shard_map/ppermute | solution.py:36
  59.4 26.6 %collective-permute-done.1 = bf16[1024,256]{1,0:T(8,128)(2,1)S(1)} collective-permute-done((bf16[1024,256]{1,0:T(8,128)(2,1)}, bf16[1024,256]{1,0:T(8,128)(2,1)S(1)}, u32[]{:S(2)}, u32[]{:S(2)}) %collective-permute-start.1) | collective-permute-done | bytes 524320 | tf_op jit(solution)/shard_map/ppermute | solution.py:36
  86.0 27.8 %collective-permute-done = bf16[1024,256]{1,0:T(8,128)(2,1)S(1)} collective-permute-done((bf16[1024,256]{1,0:T(8,128)(2,1)}, bf16[1024,256]{1,0:T(8,128)(2,1)S(1)}, u32[]{:S(2)}, u32[]{:S(2)}) %collective-permute-start) | collective-permute-done | bytes 524320 | tf_op jit(solution)/shard_map/ppermute | solution.py:36
  113.8 1.2 pad_maximum_fusion
  115.0 0.1 fusion.6
  115.1 0.0 all-to-all-done
  115.1 1.7 fusion.7
  116.8 33.6 %shard_map.85 = (bf16[1024,512]{1,0:T(8,128)(2,1)S(1)}, f32[4096,256]{1,0:T(8,128)}) custom-call(s32[8]{0:T(128)S(1)} %pad_add_fusion.1.meta_ref, bf16[1024,512]{1,0:T(8,128)(2,1)S(1)} %get-tuple-element.21.q_ref, bf16[1024,512]{1,0:T(8,128)(2,1)S(1)} %get-tuple-element.20.do_ref, bf16[4096,128]{1,0:T(8,128)(2,1)S(1)} %get-tuple-element.19.k_ref, ...), custom_call_target="tpu_custom_call" | custom-call | tf_op jit(solution)/shard_map/pallas_call | solution.py:156
  150.4 1.0 copy-done
  151.4 2.3 copy.29
  153.6 3.6 %all-to-all-start.2 = ((bf16[8,128,512]{1,2,0:T(8,128)(2,1)}), bf16[8,128,512]{1,2,0:T(8,128)(2,1)S(1)}, u32[]{:S(2)}, u32[]{:S(2)}) async-start(bf16[8,128,512]{1,2,0:T(8,128)(2,1)} %copy.29), calls=%async_computation.2 | async-start | bytes 2097152 | tf_op jit(solution)/shard_map/all_to_all | solution.py:235
  157.2 2.4 convert.8
  159.6 0.1 fusion.5
  159.7 9.2 %collective-permute-start.5 = (bf16[1024,256]{1,0:T(8,128)(2,1)S(1)}, bf16[1024,256]{1,0:T(8,128)(2,1)S(1)}, u32[]{:S(2)}, u32[]{:S(2)}) collective-permute-start(bf16[1024,256]{1,0:T(8,128)(2,1)S(1)} %get-tuple-element.15), channel_id=1, source_target_pairs={{24,0},{25,1},{26,2},{27,3},{28,4},{29,5},{30,6},{31,7},{32,14},{3... | collective-permute-start | bytes 1572872 | tf_op jit(solution)/shard_map/ppermute | solution.py:36
  169.0 41.5 %collective-permute-start.4 = (bf16[1024,256]{1,0:T(8,128)(2,1)S(1)}, bf16[1024,256]{1,0:T(8,128)(2,1)S(1)}, u32[]{:S(2)}, u32[]{:S(2)}) collective-permute-start(bf16[1024,256]{1,0:T(8,128)(2,1)S(1)} %get-tuple-element.16), channel_id=1, source_target_pairs={{16,0},{17,1},{18,2},{19,3},{20,4},{21,5},{22,6},{23,7},{24,8},{25... | collective-permute-start | bytes 1572872 | tf_op jit(solution)/shard_map/ppermute | solution.py:36
  210.5 1.9 collective-permute-start.3
  212.4 0.0 collective-permute-done.5
  212.4 10.3 %collective-permute-done.4 = bf16[1024,256]{1,0:T(8,128)(2,1)S(1)} collective-permute-done((bf16[1024,256]{1,0:T(8,128)(2,1)S(1)}, bf16[1024,256]{1,0:T(8,128)(2,1)S(1)}, u32[]{:S(2)}, u32[]{:S(2)}) %collective-permute-start.4) | collective-permute-done | bytes 524320 | tf_op jit(solution)/shard_map/ppermute | solution.py:36
  222.7 56.9 %collective-permute-done.3 = bf16[1024,256]{1,0:T(8,128)(2,1)S(1)} collective-permute-done((bf16[1024,256]{1,0:T(8,128)(2,1)S(1)}, bf16[1024,256]{1,0:T(8,128)(2,1)S(1)}, u32[]{:S(2)}, u32[]{:S(2)}) %collective-permute-start.3) | collective-permute-done | bytes 524320 | tf_op jit(solution)/shard_map/ppermute | solution.py:36
  279.7 0.0 all-to-all-done.2
  279.7 1.4 convert_add_fusion
  281.2 0.8 pad_maximum_fusion.1
  282.1 4.7 %all-to-all-start.3 = ((bf16[8,128,256]{2,1,0:T(8,128)(2,1)}), bf16[8,128,256]{2,1,0:T(8,128)(2,1)S(1)}, u32[]{:S(2)}, u32[]{:S(2)}) async-start(bf16[8,128,256]{2,1,0:T(8,128)(2,1)} %bitcast.27), calls=%async_computation.3 | async-start | bytes 1048576 | tf_op jit(solution)/shard_map/all_to_all | solution.py:243
  286.8 0.8 reverse_select_fusion
  287.7 1.3 copy.33
  289.0 13.2 %all-to-all-done.3 = bf16[8,128,256]{2,1,0:T(8,128)(2,1)S(1)} async-done(((bf16[8,128,256]{2,1,0:T(8,128)(2,1)}), bf16[8,128,256]{2,1,0:T(8,128)(2,1)S(1)}, u32[]{:S(2)}, u32[]{:S(2)}) %all-to-all-start.3) | async-done | bytes 524320 | tf_op jit(solution)/shard_map/all_to_all | solution.py:243
  302.2 0.5 copy.31
  302.7 1.2 broadcast_select_fusion.1
  303.9 0.2 reshape.233
  304.1 0.8 copy.38
  304.9 0.8 copy.39
  (11 shorter events, 0.2 us)
Async XLA Ops:
  1.9 10.8 %copy-start.1 = (bf16[128,4096]{1,0:T(8,128)(2,1)S(1)}, bf16[128,4096]{1,0:T(8,128)(2,1)}, u32[]{:S(2)}) copy-start(bf16[128,4096]{1,0:T(8,128)(2,1)} %param.6) | copy-start | bytes 3145732
  6.9 21.4 %all-to-all-start.1 = ((bf16[128,8,256]{2,0,1:T(8,128)(2,1)}), bf16[128,8,256]{2,0,1:T(8,128)(2,1)}, u32[]{:S(2)}, u32[]{:S(2)}) async-start(bf16[128,8,256]{2,0,1:T(8,128)(2,1)} %bitcast.14), calls=%async_computation.1 | async-start | bytes 1048576 | tf_op jit(solution)/shard_map/all_to_all | solution.py:187
  28.2 4.5 %copy-start.2 = (s32[32]{0:T(128)S(1)}, s32[32]{0:T(128)}, u32[]{:S(2)}) copy-start(s32[32]{0:T(128)} %param.10) | copy-start | bytes 388
  28.2 86.9 %all-to-all-start = ((bf16[128,8,1024]{2,0,1:T(8,128)(2,1)}), bf16[128,8,1024]{2,0,1:T(8,128)(2,1)}, u32[]{:S(2)}, u32[]{:S(2)}) async-start(bf16[128,8,1024]{2,0,1:T(8,128)(2,1)} %bitcast.8), calls=%async_computation | async-start | bytes 4194304 | tf_op jit(solution)/shard_map/all_to_all | solution.py:198
  34.4 25.0 %collective-permute-start.2 = (bf16[1024,256]{1,0:T(8,128)(2,1)}, bf16[1024,256]{1,0:T(8,128)(2,1)S(1)}, u32[]{:S(2)}, u32[]{:S(2)}) collective-permute-start(bf16[1024,256]{1,0:T(8,128)(2,1)} %bitcast.17), channel_id=1, source_target_pairs={{0,8},{1,9},{2,10},{3,11},{4,12},{5,13},{6,14},{7,15},{8,16},{9,17... | collective-permute-start | bytes 1572872 | tf_op jit(solution)/shard_map/ppermute | solution.py:36
  42.0 44.0 %collective-permute-start.1 = (bf16[1024,256]{1,0:T(8,128)(2,1)}, bf16[1024,256]{1,0:T(8,128)(2,1)S(1)}, u32[]{:S(2)}, u32[]{:S(2)}) collective-permute-start(bf16[1024,256]{1,0:T(8,128)(2,1)} %bitcast.17), channel_id=1, source_target_pairs={{0,16},{1,17},{2,18},{3,19},{4,20},{5,21},{6,22},{7,23},{8,24},{9,... | collective-permute-start | bytes 1572872 | tf_op jit(solution)/shard_map/ppermute | solution.py:36
  46.3 67.4 %collective-permute-start = (bf16[1024,256]{1,0:T(8,128)(2,1)}, bf16[1024,256]{1,0:T(8,128)(2,1)S(1)}, u32[]{:S(2)}, u32[]{:S(2)}) collective-permute-start(bf16[1024,256]{1,0:T(8,128)(2,1)} %bitcast.17), channel_id=1, source_target_pairs={{0,24},{1,25},{2,26},{3,27},{4,28},{5,29},{6,30},{7,31},{8,38},{9,... | collective-permute-start | bytes 1572872 | tf_op jit(solution)/shard_map/ppermute | solution.py:36
  150.4 1.0 copy-start
  153.6 126.0 %all-to-all-start.2 = ((bf16[8,128,512]{1,2,0:T(8,128)(2,1)}), bf16[8,128,512]{1,2,0:T(8,128)(2,1)S(1)}, u32[]{:S(2)}, u32[]{:S(2)}) async-start(bf16[8,128,512]{1,2,0:T(8,128)(2,1)} %copy.29), calls=%async_computation.2 | async-start | bytes 2097152 | tf_op jit(solution)/shard_map/all_to_all | solution.py:235
  159.7 52.7 %collective-permute-start.5 = (bf16[1024,256]{1,0:T(8,128)(2,1)S(1)}, bf16[1024,256]{1,0:T(8,128)(2,1)S(1)}, u32[]{:S(2)}, u32[]{:S(2)}) collective-permute-start(bf16[1024,256]{1,0:T(8,128)(2,1)S(1)} %get-tuple-element.15), channel_id=1, source_target_pairs={{24,0},{25,1},{26,2},{27,3},{28,4},{29,5},{30,6},{31,7},{32,14},{3... | collective-permute-start | bytes 1572872 | tf_op jit(solution)/shard_map/ppermute | solution.py:36
  169.0 53.8 %collective-permute-start.4 = (bf16[1024,256]{1,0:T(8,128)(2,1)S(1)}, bf16[1024,256]{1,0:T(8,128)(2,1)S(1)}, u32[]{:S(2)}, u32[]{:S(2)}) collective-permute-start(bf16[1024,256]{1,0:T(8,128)(2,1)S(1)} %get-tuple-element.16), channel_id=1, source_target_pairs={{16,0},{17,1},{18,2},{19,3},{20,4},{21,5},{22,6},{23,7},{24,8},{25... | collective-permute-start | bytes 1572872 | tf_op jit(solution)/shard_map/ppermute | solution.py:36
  210.5 69.2 %collective-permute-start.3 = (bf16[1024,256]{1,0:T(8,128)(2,1)S(1)}, bf16[1024,256]{1,0:T(8,128)(2,1)S(1)}, u32[]{:S(2)}, u32[]{:S(2)}) collective-permute-start(bf16[1024,256]{1,0:T(8,128)(2,1)S(1)} %get-tuple-element.17), channel_id=1, source_target_pairs={{8,0},{9,1},{10,2},{11,3},{12,4},{13,5},{14,6},{15,7},{16,8},{17,9... | collective-permute-start | bytes 1572872 | tf_op jit(solution)/shard_map/ppermute | solution.py:36
  282.1 20.1 %all-to-all-start.3 = ((bf16[8,128,256]{2,1,0:T(8,128)(2,1)}), bf16[8,128,256]{2,1,0:T(8,128)(2,1)S(1)}, u32[]{:S(2)}, u32[]{:S(2)}) async-start(bf16[8,128,256]{2,1,0:T(8,128)(2,1)} %bitcast.27), calls=%async_computation.3 | async-start | bytes 1048576 | tf_op jit(solution)/shard_map/all_to_all | solution.py:243
where the time goes:
time: 305 us; the launch traced here: 306 us
  waiting for transfers between devices  151 us (50%)
  starting transfers between devices  85.2 us (28%)
  Pallas kernels  33.6 us (11%)
  local copies, waits for them, and re-layouts  22.8 us (7%)
  other arithmetic  12.3 us (4%)
    ppermute x6, waiting for transfers between devices, from_behind(): return lax.ppermute(shard, ('ctx', 'uly'), pairs)  132 us
    ppermute x6, starting transfers between devices, from_behind(): return lax.ppermute(shard, ('ctx', 'uly'), pairs)  66.5 us
    pallas_call x1, Pallas kernels, attend(): pl.pallas_call(kernel, out_shape=(jax.ShapeDtypeStruct(queries.shape, jnp...  33.6 us
    all_to_all x1, waiting for transfers between devices, on_device(): lax.all_to_all(jnp.concatenate([out_k, out_v], axis=1), 'uly', split_axis...  13.2 us
  transfers between devices with their start and end apart: 10, of which 7 were waited for; matrix products, arithmetic and copies ran while one was open for 6% of the time, Pallas kernels for 0%

commit v1 on v0

--- a/solution.py
+++ b/solution.py
@@ -189,7 +189,8 @@
     kv = kv.reshape(rows, 2 * kv_cols)
     window = [kv]
     for step in range(1, REACH + 1):
-        window.append(from_behind(kv, step, flips, cores))
+        source = window[1] if step == 2 else kv
+        window.append(from_behind(source, 1 if step == 2 else step, flips, cores))
     packed = jnp.concatenate(
         [queries.reshape(tokens, uly, q_cols), output_gradient.reshape(tokens, uly, q_cols)],
         axis=2,

time: 305 us -> 278 us (0.911)
  waiting for transfers between devices: 151 us -> 131 us
  starting transfers between devices: 85.2 us -> 81.2 us
    ppermute x6, waiting for transfers between devices: 132 us -> 113 us  [from_behind(): return lax.ppermute(shard, ('ctx', 'uly'), pairs)]
    ppermute x6, starting transfers between devices: 66.5 us -> 60.9 us  [from_behind(): return lax.ppermute(shard, ('ctx', 'uly'), pairs)]
where the time goes in v1:
time: 278 us; the launch traced here: 282 us
  waiting for transfers between devices  131 us (47%)
  starting transfers between devices  81.2 us (29%)
  Pallas kernels  33.3 us (12%)
  local copies, waits for them, and re-layouts  22.8 us (8%)
  other arithmetic  12.3 us (4%)
    ppermute x6, waiting for transfers between devices, from_behind(): return lax.ppermute(shard, ('ctx', 'uly'), pairs)  113 us
    ppermute x6, starting transfers between devices, from_behind(): return lax.ppermute(shard, ('ctx', 'uly'), pairs)  60.9 us
    pallas_call x1, Pallas kernels, attend(): pl.pallas_call(kernel, out_shape=(jax.ShapeDtypeStruct(queries.shape, jnp...  33.3 us
    all_to_all x1, waiting for transfers between devices, on_device(): lax.all_to_all(jnp.concatenate([out_k, out_v], axis=1), 'uly', split_axis...  13.2 us
    all_to_all x1, starting transfers between devices, on_device(): lax.all_to_all(jnp.concatenate([out_k, out_v], axis=1), 'uly', split_axis...  6.34 us
    select_n x4, other arithmetic, mirrored(): return jnp.where(flip, split[:, ::-1], split).reshape(x.shape)  5.99 us
    all_to_all x1, starting transfers between devices, on_device(): lax.all_to_all(mirrored(kv, flip, cores), 'uly', split_axis=1, concat_axi...  5.9 us
  transfers between devices with their start and end apart: 10, of which 7 were waited for; matrix products, arithmetic and copies ran while one was open for 6% of the time, Pallas kernels for 0%

profile of v1, /device:TPU:22, one launch (start us, length us, event | category | flops | bytes accessed | tf_op | source)
XLA Modules:
  0.0 281.6 jit_solution(12473415289460611532)
XLA Ops:
  0.6 1.1 concatenate.29
  1.8 0.2 constant_dynamic-update-slice_fusion.3
  1.9 0.0 copy-start.1
  2.0 1.2 concatenate.30
  3.2 1.3 dynamic_slice.3
  4.4 0.4 constant_dynamic-update-slice_fusion.2
  4.8 1.2 broadcast_select_fusion.2
  6.0 0.9 copy.27
  6.9 5.9 %all-to-all-start.1 = ((bf16[128,8,256]{2,0,1:T(8,128)(2,1)}), bf16[128,8,256]{2,0,1:T(8,128)(2,1)}, u32[]{:S(2)}, u32[]{:S(2)}) async-start(bf16[128,8,256]{2,0,1:T(8,128)(2,1)} %bitcast.14), calls=%async_computation.1 | async-start | bytes 1048576 | tf_op jit(solution)/shard_map/all_to_all | solution.py:187
  12.8 0.0 copy-done.1
  12.8 0.8 concatenate.26
  13.6 1.2 constant_dynamic-update-slice_fusion.1
  14.8 1.8 concatenate.27
  16.6 0.9 constant_dynamic-update-slice_fusion
  17.6 2.8 broadcast_select_fusion
  20.4 2.5 copy.26
  22.8 5.4 %all-to-all-done.1 = bf16[128,8,256]{2,0,1:T(8,128)(2,1)} async-done(((bf16[128,8,256]{2,0,1:T(8,128)(2,1)}), bf16[128,8,256]{2,0,1:T(8,128)(2,1)}, u32[]{:S(2)}, u32[]{:S(2)}) %all-to-all-start.1) | async-done | bytes 524320 | tf_op jit(solution)/shard_map/all_to_all | solution.py:187
  28.2 0.0 copy-start.2
  28.2 4.5 %all-to-all-start = ((bf16[128,8,1024]{2,0,1:T(8,128)(2,1)}), bf16[128,8,1024]{2,0,1:T(8,128)(2,1)}, u32[]{:S(2)}, u32[]{:S(2)}) async-start(bf16[128,8,1024]{2,0,1:T(8,128)(2,1)} %bitcast.8), calls=%async_computation | async-start | bytes 4194304 | tf_op jit(solution)/shard_map/all_to_all | solution.py:199
  32.7 0.0 copy-done.2
  32.8 0.1 copy.24
  32.8 0.1 reduce-window.8
  32.9 0.1 reduce
  33.0 7.6 %collective-permute-start.1 = (bf16[1024,256]{1,0:T(8,128)(2,1)}, bf16[1024,256]{1,0:T(8,128)(2,1)S(1)}, u32[]{:S(2)}, u32[]{:S(2)}) collective-permute-start(bf16[1024,256]{1,0:T(8,128)(2,1)} %bitcast.17), channel_id=1, source_target_pairs={{0,8},{1,9},{2,10},{3,11},{4,12},{5,13},{6,14},{7,15},{8,16},{9,17... | collective-permute-start | bytes 1572872 | tf_op jit(solution)/shard_map/ppermute | solution.py:36
  40.7 0.1 select_reduce_fusion
  40.8 0.6 gather_fusion.1
  41.4 0.6 gather_fusion
  42.0 3.4 %collective-permute-start = (bf16[1024,256]{1,0:T(8,128)(2,1)}, bf16[1024,256]{1,0:T(8,128)(2,1)S(1)}, u32[]{:S(2)}, u32[]{:S(2)}) collective-permute-start(bf16[1024,256]{1,0:T(8,128)(2,1)} %bitcast.17), channel_id=1, source_target_pairs={{0,24},{1,25},{2,26},{3,27},{4,28},{5,29},{6,30},{7,31},{8,38},{9,... | collective-permute-start | bytes 1572872 | tf_op jit(solution)/shard_map/ppermute | solution.py:36
  45.5 7.7 %collective-permute-done.1 = bf16[1024,256]{1,0:T(8,128)(2,1)S(1)} collective-permute-done((bf16[1024,256]{1,0:T(8,128)(2,1)}, bf16[1024,256]{1,0:T(8,128)(2,1)S(1)}, u32[]{:S(2)}, u32[]{:S(2)}) %collective-permute-start.1) | collective-permute-done | bytes 524320 | tf_op jit(solution)/shard_map/ppermute | solution.py:36
  53.2 7.6 %collective-permute-start.2 = (bf16[1024,256]{1,0:T(8,128)(2,1)S(1)}, bf16[1024,256]{1,0:T(8,128)(2,1)S(1)}, u32[]{:S(2)}, u32[]{:S(2)}) collective-permute-start(bf16[1024,256]{1,0:T(8,128)(2,1)S(1)} %collective-permute-done.1), channel_id=1, source_target_pairs={{0,8},{1,9},{2,10},{3,11},{4,12},{5,13},{6,14},{7,15},{8,16},{9,17... | collective-permute-start | bytes 1572872 | tf_op jit(solution)/shard_map/ppermute | solution.py:36
  60.9 0.1 copy.25
  60.9 0.1 reshape.228
  61.0 0.2 copy.28.qs_ref
  61.3 0.1 pad_add_fusion.1.meta_ref
  61.3 15.1 %collective-permute-done = bf16[1024,256]{1,0:T(8,128)(2,1)S(1)} collective-permute-done((bf16[1024,256]{1,0:T(8,128)(2,1)}, bf16[1024,256]{1,0:T(8,128)(2,1)S(1)}, u32[]{:S(2)}, u32[]{:S(2)}) %collective-permute-start) | collective-permute-done | bytes 524320 | tf_op jit(solution)/shard_map/ppermute | solution.py:36
  76.4 32.0 %collective-permute-done.2 = bf16[1024,256]{1,0:T(8,128)(2,1)S(1)} collective-permute-done((bf16[1024,256]{1,0:T(8,128)(2,1)S(1)}, bf16[1024,256]{1,0:T(8,128)(2,1)S(1)}, u32[]{:S(2)}, u32[]{:S(2)}) %collective-permute-start.2) | collective-permute-done | bytes 524320 | tf_op jit(solution)/shard_map/ppermute | solution.py:36
  108.5 1.2 pad_maximum_fusion
  109.7 0.1 fusion.6
  109.8 0.0 all-to-all-done
  109.8 1.7 fusion.7
  111.5 33.3 %shard_map.85 = (bf16[1024,512]{1,0:T(8,128)(2,1)S(1)}, f32[4096,256]{1,0:T(8,128)}) custom-call(s32[8]{0:T(128)S(1)} %pad_add_fusion.1.meta_ref, bf16[1024,512]{1,0:T(8,128)(2,1)S(1)} %get-tuple-element.21.q_ref, bf16[1024,512]{1,0:T(8,128)(2,1)S(1)} %get-tuple-element.20.do_ref, bf16[4096,128]{1,0:T(8,128)(2,1)S(1)} %get-tuple-element.19.k_ref, ...), custom_call_target="tpu_custom_call" | custom-call | tf_op jit(solution)/shard_map/pallas_call | solution.py:156
  144.8 1.0 copy-done
  145.7 2.3 copy.29
  148.0 3.6 %all-to-all-start.2 = ((bf16[8,128,512]{1,2,0:T(8,128)(2,1)}), bf16[8,128,512]{1,2,0:T(8,128)(2,1)S(1)}, u32[]{:S(2)}, u32[]{:S(2)}) async-start(bf16[8,128,512]{1,2,0:T(8,128)(2,1)} %copy.29), calls=%async_computation.2 | async-start | bytes 2097152 | tf_op jit(solution)/shard_map/all_to_all | solution.py:236
  151.6 2.4 convert.8
  154.0 0.1 fusion.5
  154.1 7.8 %collective-permute-start.5 = (bf16[1024,256]{1,0:T(8,128)(2,1)S(1)}, bf16[1024,256]{1,0:T(8,128)(2,1)S(1)}, u32[]{:S(2)}, u32[]{:S(2)}) collective-permute-start(bf16[1024,256]{1,0:T(8,128)(2,1)S(1)} %get-tuple-element.15), channel_id=1, source_target_pairs={{24,0},{25,1},{26,2},{27,3},{28,4},{29,5},{30,6},{31,7},{32,14},{3... | collective-permute-start | bytes 1572872 | tf_op jit(solution)/shard_map/ppermute | solution.py:36
  161.9 16.0 %collective-permute-start.4 = (bf16[1024,256]{1,0:T(8,128)(2,1)S(1)}, bf16[1024,256]{1,0:T(8,128)(2,1)S(1)}, u32[]{:S(2)}, u32[]{:S(2)}) collective-permute-start(bf16[1024,256]{1,0:T(8,128)(2,1)S(1)} %get-tuple-element.16), channel_id=1, source_target_pairs={{16,0},{17,1},{18,2},{19,3},{20,4},{21,5},{22,6},{23,7},{24,8},{25... | collective-permute-start | bytes 1572872 | tf_op jit(solution)/shard_map/ppermute | solution.py:36
  177.9 18.4 %collective-permute-start.3 = (bf16[1024,256]{1,0:T(8,128)(2,1)S(1)}, bf16[1024,256]{1,0:T(8,128)(2,1)S(1)}, u32[]{:S(2)}, u32[]{:S(2)}) collective-permute-start(bf16[1024,256]{1,0:T(8,128)(2,1)S(1)} %get-tuple-element.17), channel_id=1, source_target_pairs={{8,0},{9,1},{10,2},{11,3},{12,4},{13,5},{14,6},{15,7},{16,8},{17,9... | collective-permute-start | bytes 1572872 | tf_op jit(solution)/shard_map/ppermute | solution.py:36
  196.3 0.0 collective-permute-done.5
  196.4 46.5 %collective-permute-done.4 = bf16[1024,256]{1,0:T(8,128)(2,1)S(1)} collective-permute-done((bf16[1024,256]{1,0:T(8,128)(2,1)S(1)}, bf16[1024,256]{1,0:T(8,128)(2,1)S(1)}, u32[]{:S(2)}, u32[]{:S(2)}) %collective-permute-start.4) | collective-permute-done | bytes 524320 | tf_op jit(solution)/shard_map/ppermute | solution.py:36
  242.8 11.2 %collective-permute-done.3 = bf16[1024,256]{1,0:T(8,128)(2,1)S(1)} collective-permute-done((bf16[1024,256]{1,0:T(8,128)(2,1)S(1)}, bf16[1024,256]{1,0:T(8,128)(2,1)S(1)}, u32[]{:S(2)}, u32[]{:S(2)}) %collective-permute-start.3) | collective-permute-done | bytes 524320 | tf_op jit(solution)/shard_map/ppermute | solution.py:36
  254.0 0.0 all-to-all-done.2
  254.0 1.4 convert_add_fusion
  255.5 0.8 pad_maximum_fusion.1
  256.4 6.3 %all-to-all-start.3 = ((bf16[8,128,256]{2,1,0:T(8,128)(2,1)}), bf16[8,128,256]{2,1,0:T(8,128)(2,1)S(1)}, u32[]{:S(2)}, u32[]{:S(2)}) async-start(bf16[8,128,256]{2,1,0:T(8,128)(2,1)} %bitcast.27), calls=%async_computation.3 | async-start | bytes 1048576 | tf_op jit(solution)/shard_map/all_to_all | solution.py:244
  262.7 0.8 reverse_select_fusion
  263.6 1.3 copy.33
  264.9 13.2 %all-to-all-done.3 = bf16[8,128,256]{2,1,0:T(8,128)(2,1)S(1)} async-done(((bf16[8,128,256]{2,1,0:T(8,128)(2,1)}), bf16[8,128,256]{2,1,0:T(8,128)(2,1)S(1)}, u32[]{:S(2)}, u32[]{:S(2)}) %all-to-all-start.3) | async-done | bytes 524320 | tf_op jit(solution)/shard_map/all_to_all | solution.py:244
  278.1 0.5 copy.31
  278.6 1.2 broadcast_select_fusion.1
  279.8 0.2 reshape.233
  280.1 0.8 copy.38
  280.8 0.8 copy.39
  (11 shorter events, 0.2 us)
Async XLA Ops:
  1.9 10.8 %copy-start.1 = (bf16[128,4096]{1,0:T(8,128)(2,1)S(1)}, bf16[128,4096]{1,0:T(8,128)(2,1)}, u32[]{:S(2)}) copy-start(bf16[128,4096]{1,0:T(8,128)(2,1)} %param.6) | copy-start | bytes 3145732
  6.9 21.4 %all-to-all-start.1 = ((bf16[128,8,256]{2,0,1:T(8,128)(2,1)}), bf16[128,8,256]{2,0,1:T(8,128)(2,1)}, u32[]{:S(2)}, u32[]{:S(2)}) async-start(bf16[128,8,256]{2,0,1:T(8,128)(2,1)} %bitcast.14), calls=%async_computation.1 | async-start | bytes 1048576 | tf_op jit(solution)/shard_map/all_to_all | solution.py:187
  28.2 4.5 %copy-start.2 = (s32[32]{0:T(128)S(1)}, s32[32]{0:T(128)}, u32[]{:S(2)}) copy-start(s32[32]{0:T(128)} %param.10) | copy-start | bytes 388
  28.2 81.6 %all-to-all-start = ((bf16[128,8,1024]{2,0,1:T(8,128)(2,1)}), bf16[128,8,1024]{2,0,1:T(8,128)(2,1)}, u32[]{:S(2)}, u32[]{:S(2)}) async-start(bf16[128,8,1024]{2,0,1:T(8,128)(2,1)} %bitcast.8), calls=%async_computation | async-start | bytes 4194304 | tf_op jit(solution)/shard_map/all_to_all | solution.py:199
  33.0 20.2 %collective-permute-start.1 = (bf16[1024,256]{1,0:T(8,128)(2,1)}, bf16[1024,256]{1,0:T(8,128)(2,1)S(1)}, u32[]{:S(2)}, u32[]{:S(2)}) collective-permute-start(bf16[1024,256]{1,0:T(8,128)(2,1)} %bitcast.17), channel_id=1, source_target_pairs={{0,8},{1,9},{2,10},{3,11},{4,12},{5,13},{6,14},{7,15},{8,16},{9,17... | collective-permute-start | bytes 1572872 | tf_op jit(solution)/shard_map/ppermute | solution.py:36
  42.0 34.4 %collective-permute-start = (bf16[1024,256]{1,0:T(8,128)(2,1)}, bf16[1024,256]{1,0:T(8,128)(2,1)S(1)}, u32[]{:S(2)}, u32[]{:S(2)}) collective-permute-start(bf16[1024,256]{1,0:T(8,128)(2,1)} %bitcast.17), channel_id=1, source_target_pairs={{0,24},{1,25},{2,26},{3,27},{4,28},{5,29},{6,30},{7,31},{8,38},{9,... | collective-permute-start | bytes 1572872 | tf_op jit(solution)/shard_map/ppermute | solution.py:36
  53.2 55.3 %collective-permute-start.2 = (bf16[1024,256]{1,0:T(8,128)(2,1)S(1)}, bf16[1024,256]{1,0:T(8,128)(2,1)S(1)}, u32[]{:S(2)}, u32[]{:S(2)}) collective-permute-start(bf16[1024,256]{1,0:T(8,128)(2,1)S(1)} %collective-permute-done.1), channel_id=1, source_target_pairs={{0,8},{1,9},{2,10},{3,11},{4,12},{5,13},{6,14},{7,15},{8,16},{9,17... | collective-permute-start | bytes 1572872 | tf_op jit(solution)/shard_map/ppermute | solution.py:36
  144.8 1.0 copy-start
  148.0 106.0 %all-to-all-start.2 = ((bf16[8,128,512]{1,2,0:T(8,128)(2,1)}), bf16[8,128,512]{1,2,0:T(8,128)(2,1)S(1)}, u32[]{:S(2)}, u32[]{:S(2)}) async-start(bf16[8,128,512]{1,2,0:T(8,128)(2,1)} %copy.29), calls=%async_computation.2 | async-start | bytes 2097152 | tf_op jit(solution)/shard_map/all_to_all | solution.py:236
  154.1 42.3 %collective-permute-start.5 = (bf16[1024,256]{1,0:T(8,128)(2,1)S(1)}, bf16[1024,256]{1,0:T(8,128)(2,1)S(1)}, u32[]{:S(2)}, u32[]{:S(2)}) collective-permute-start(bf16[1024,256]{1,0:T(8,128)(2,1)S(1)} %get-tuple-element.15), channel_id=1, source_target_pairs={{24,0},{25,1},{26,2},{27,3},{28,4},{29,5},{30,6},{31,7},{32,14},{3... | collective-permute-start | bytes 1572872 | tf_op jit(solution)/shard_map/ppermute | solution.py:36
  161.9 80.9 %collective-permute-start.4 = (bf16[1024,256]{1,0:T(8,128)(2,1)S(1)}, bf16[1024,256]{1,0:T(8,128)(2,1)S(1)}, u32[]{:S(2)}, u32[]{:S(2)}) collective-permute-start(bf16[1024,256]{1,0:T(8,128)(2,1)S(1)} %get-tuple-element.16), channel_id=1, source_target_pairs={{16,0},{17,1},{18,2},{19,3},{20,4},{21,5},{22,6},{23,7},{24,8},{25... | collective-permute-start | bytes 1572872 | tf_op jit(solution)/shard_map/ppermute | solution.py:36
  177.9 76.0 %collective-permute-start.3 = (bf16[1024,256]{1,0:T(8,128)(2,1)S(1)}, bf16[1024,256]{1,0:T(8,128)(2,1)S(1)}, u32[]{:S(2)}, u32[]{:S(2)}) collective-permute-start(bf16[1024,256]{1,0:T(8,128)(2,1)S(1)} %get-tuple-element.17), channel_id=1, source_target_pairs={{8,0},{9,1},{10,2},{11,3},{12,4},{13,5},{14,6},{15,7},{16,8},{17,9... | collective-permute-start | bytes 1572872 | tf_op jit(solution)/shard_map/ppermute | solution.py:36
  256.4 21.7 %all-to-all-start.3 = ((bf16[8,128,256]{2,1,0:T(8,128)(2,1)}), bf16[8,128,256]{2,1,0:T(8,128)(2,1)S(1)}, u32[]{:S(2)}, u32[]{:S(2)}) async-start(bf16[8,128,256]{2,1,0:T(8,128)(2,1)} %bitcast.27), calls=%async_computation.3 | async-start | bytes 1048576 | tf_op jit(solution)/shard_map/all_to_all | solution.py:244
